TPU v7x, 512 devices: a whole 4x4x16 slice. The times are simulated.
512 devices in a mesh: aux: 16 (over z), pair: 32 (over y, x, core).
Axes of the slice: x: 4, y: 4, z: 16, core: 2. Of those that a mesh axis runs over, the one named last changes fastest.
Arguments:
- b_tensor: bfloat16 [2560, 262144], P('aux', 'pair'), may hold values from -0.0625 to 0.0625
- eps_occ: float32 [256], replicated, may hold values from -1 to -0.3
- eps_vir: float32 [1024], replicated, may hold values from 0.05 to 3
- trial: bfloat16 [32, 262144], P(None, 'pair'), may hold values from -6 to 6
Outputs:
- trial_next: float32 [32, 262144], P(None, 'pair')
- residual: bfloat16 [32, 262144], P(None, 'pair')
- subspace: float32 [32, 32], replicated
All inputs are finite; a program needn't handle non-finite values.
Results may differ from a plain program's by a relative error of at most 0.028.
Values may be sent and summed in bfloat16 or wider, within the bound.
No kernel may reach another device: no remote copies, remote signals or barrier semaphores. Data moves between devices by JAX's collectives and lax.ppermute only.
A program may use at most 64 MiB of HBM per device.

v0:
```python
import jax
import jax.numpy as jnp
from jax import lax
from jax.sharding import PartitionSpec as P

ITERS = 2
HIGHEST_PRECISION = lax.Precision.HIGHEST


def correlation_of(first_rows, second_rows, precision=HIGHEST_PRECISION):
    return lax.dot_general(
        first_rows,
        second_rows,
        (((1,), (1,)), ((), ())),
        precision=precision,
        preferred_element_type=jnp.float32,
    )


def product(first_mat, second_mat):
    return jnp.dot(
        first_mat, second_mat, precision=HIGHEST_PRECISION, preferred_element_type=jnp.float32
    )


def pair_sum(matrices):
    return lax.all_gather(matrices, "pair").sum(0)


def aux_sum(terms):
    n_aux = lax.axis_size("aux")
    rows, cols = terms.shape
    pieces = terms.reshape(rows, n_aux, cols // n_aux)
    pieces = lax.all_to_all(pieces, "aux", 1, 1, tiled=True)
    mine = pieces.astype(jnp.float32).sum(1)
    return lax.all_gather(mine, "aux", axis=1, tiled=True)


def inverse_factor(gram_now):
    lower_tri = jnp.linalg.cholesky(gram_now)
    return lax.linalg.triangular_solve(
        lower_tri, jnp.eye(gram_now.shape[0], dtype=jnp.float32), left_side=True, lower=True
    )


def on_device(b_tensor, eps_occ, eps_vir, trial):
    block_cols = b_tensor.shape[1]
    npair_all = eps_occ.shape[0] * eps_vir.shape[0]
    k = trial.shape[0]
    everything = (eps_vir[None, :] - eps_occ[:, None]).reshape(npair_all)
    diagonal = lax.dynamic_slice_in_dim(everything, lax.axis_index("pair") * block_cols, block_cols)
    diag_row = diagonal[None, :]
    trial_now = trial
    for iteration in range(ITERS):
        if iteration == 0:
            gram_part = correlation_of(trial_now, trial_now, None)
            cross_part = correlation_of(b_tensor, trial_now, None)
        else:
            gram_part = correlation_of(trial_now, trial_now)
            cross_part = correlation_of(b_tensor.astype(jnp.float32), trial_now)
        summed = pair_sum(jnp.concatenate([gram_part / npair_all, cross_part], axis=0))
        inverse = inverse_factor(summed[:k])
        basis_now = product(inverse, trial_now.astype(jnp.float32))
        projected = lax.dot_general(
            summed[k:],
            inverse,
            (((1,), (1,)), ((), ())),
            precision=HIGHEST_PRECISION,
            preferred_element_type=jnp.float32,
        )
        projected_low = projected.astype(jnp.bfloat16)
        term = lax.dot_general(
            projected_low, b_tensor, (((0,), (0,)), ((), ())), preferred_element_type=jnp.float32
        ).astype(jnp.bfloat16)
        image_now = aux_sum(term) + diag_row * basis_now
        subspace = pair_sum(correlation_of(image_now, basis_now) / npair_all)
        residual = image_now - product(subspace, basis_now)
        trial_now = basis_now - residual / diag_row
    return (trial_now, residual.astype(jnp.bfloat16), subspace)


def solution(mesh):
    in_specs = (P("aux", "pair"), P(), P(), P(None, "pair"))
    out_specs = (P(None, "pair"), P(None, "pair"), P())
    return jax.shard_map(
        on_device, mesh=mesh, in_specs=in_specs, out_specs=out_specs, check_vma=False
    )
```

profile of v0, /device:TPU:1, one launch (start us, length us, event | category | flops | bytes accessed | tf_op | source)
XLA Modules:
  0.0 371.0 jit_solution(16617916019839826232)
XLA Ops:
  7.2 1.6 convolution_multiply_fusion.3
  9.2 2.0 fusion.19
  11.3 31.4 %all-gather.4 = f32[32,192,32]{1,2,0:T(8,128)} all-gather(f32[1,192,32]{1,2,0:T(8,128)S(1)} %maximum_bitcast_fusion), channel_id=2, replica_groups=mesh['aux'=16,'pair'=32] {'pair'}, dimensions={0}, use_global_device_ids=true | all-gather | bytes 811008 | tf_op jit(solution)/shard_map/all_gather | solution.py:27
  42.7 1.3 reduce_sum.54
  44.1 2.9 cholesky.44
  48.4 2.4 custom-call.6
  52.2 35.2 %all_to_all.10 = bf16[32,16,512]{2,0,1:T(8,128)(2,1)S(1)} all-to-all(bf16[32,16,512]{2,0,1:T(8,128)(2,1)S(1)} %bitcast.64), channel_id=1, replica_groups=mesh['aux'=16,'pair'=32] {'aux'}, dimensions={1} | all-to-all | bytes 1048576 | tf_op jit(solution)/shard_map/all_to_all | solution.py:34
  88.3 1.2 copy.28
  90.3 1.5 fusion.20
  91.8 57.8 %all-gather.9.cloned.1.call-done = f32[32,8192]{1,0:T(8,128)} async-done(((f32[32,512]{1,0:T(8,128)}), f32[32,8192]{1,0:T(8,128)}) %all-gather.9.cloned.1.call-update) | async-done | bytes 1048592 | tf_op jit(solution)/shard_map/all_gather | solution.py:36
  149.6 2.9 convolution_multiply_fusion.2
  152.6 34.8 %all-gather.1 = f32[1024,32]{1,0:T(8,128)S(1)} all-gather(f32[32,32]{1,0:T(8,128)S(1)} %copy.14), channel_id=3, replica_groups=mesh['aux'=16,'pair'=32] {'pair'}, dimensions={0}, use_global_device_ids=true | all-gather | bytes 135168 | tf_op jit(solution)/shard_map/all_gather | solution.py:27
  187.4 3.0 fusion.1
  190.5 2.4 convolution_bitcast_fusion
  194.0 26.7 %all-gather.5 = f32[32,192,32]{1,2,0:T(8,128)} all-gather(f32[1,192,32]{1,2,0:T(8,128)S(1)} %maximum_bitcast_fusion.1), channel_id=4, replica_groups=mesh['aux'=16,'pair'=32] {'pair'}, dimensions={0}, use_global_device_ids=true | all-gather | bytes 811008 | tf_op jit(solution)/shard_map/all_gather | solution.py:27
  220.7 1.3 reduce_sum.57
  222.1 2.9 cholesky.55
  226.3 2.4 custom-call.7
  230.1 30.5 %all_to_all.11 = bf16[32,16,512]{2,0,1:T(8,128)(2,1)S(1)} all-to-all(bf16[32,16,512]{2,0,1:T(8,128)(2,1)S(1)} %bitcast.66), channel_id=1, replica_groups=mesh['aux'=16,'pair'=32] {'aux'}, dimensions={1} | all-to-all | bytes 1048576 | tf_op jit(solution)/shard_map/all_to_all | solution.py:34
  261.3 3.2 fusion.21
  264.5 57.6 %all-gather.11.cloned.1.call-done = f32[32,8192]{1,0:T(8,128)} async-done(((f32[32,512]{1,0:T(8,128)}), f32[32,8192]{1,0:T(8,128)}) %all-gather.11.cloned.1.call-update) | async-done | bytes 1048592 | tf_op jit(solution)/shard_map/all_gather | solution.py:36
  322.1 2.9 convolution_multiply_fusion
  325.1 34.8 %all-gather.3 = f32[1024,32]{1,0:T(8,128)S(1)} all-gather(f32[32,32]{1,0:T(8,128)S(1)} %copy.19), channel_id=5, replica_groups=mesh['aux'=16,'pair'=32] {'pair'}, dimensions={0}, use_global_device_ids=true | all-gather | bytes 135168 | tf_op jit(solution)/shard_map/all_gather | solution.py:27
  360.0 4.2 %fusion.18 = (bf16[32,8192]{1,0:T(8,128)(2,1)}, f32[32,8192]{1,0:T(8,128)}) fusion(f32[32,8192]{1,0:T(8,128)} %fusion.21, f32[8192]{0:T(1024)S(1)} %dynamic_slice.3, f32[32,32]{1,0:T(8,128)S(1)} %reduce_sum.59, f32[32,8192]{1,0:T(8,128)} %all-gather.11.cloned.1.call-done), kind=kOutput, calls=%fused_computation.48 | convolution fusion | flops 102236160 | bytes 3706880 | tf_op jit(solution)/shard_map/dot_general | solution.py:21
  (47 shorter events, 9.6 us)
Async XLA Ops:
  7.2 2.1 copy-start
  7.2 142.5 %all-gather.9.cloned.1.call-start = ((), (), s32[]{:S(2)}) async-start(), calls=%async_computation.2 | async-start | bytes 1114112 | tf_op jit(solution)/shard_map/all_gather | solution.py:36
  51.4 36.7 %copy-start.4 = (f32[1024]{0:T(1024)S(1)}, f32[1024]{0:T(1024)}, u32[]{:S(2)}) copy-start(f32[1024]{0:T(1024)} %param.9) | copy-start | bytes 12292
  51.4 36.7 %copy-start.5 = (f32[256]{0:T(256)S(1)}, f32[256]{0:T(256)}, u32[]{:S(2)}) copy-start(f32[256]{0:T(256)} %param.8) | copy-start | bytes 3076
  52.2 38.1 %copy-start.2 = (bf16[32,8192]{1,0:T(8,128)(2,1)S(1)}, bf16[32,8192]{1,0:T(8,128)(2,1)}, u32[]{:S(2)}) copy-start(bf16[32,8192]{1,0:T(8,128)(2,1)} %param.10) | copy-start | bytes 1572868
  88.1 234.0 %all-gather.11.cloned.1.call-start = ((), (), s32[]{:S(2)}) async-start(), calls=%async_computation.3 | async-start | bytes 1114112 | tf_op jit(solution)/shard_map/all_gather | solution.py:36
  190.5 3.4 copy-start.1
  359.9 4.2 %copy-start.3 = (f32[32,32]{1,0:T(8,128)}, f32[32,32]{1,0:T(8,128)S(1)}, u32[]{:S(2)}) copy-start(f32[32,32]{1,0:T(8,128)S(1)} %reduce_sum.59) | copy-start | bytes 12292
Sparse Core Ops, SparseCore 0:
  88.2 61.3 all-gather.8
  261.4 60.6 all-gather.10
where the time goes:
time: 372 us; the launch traced here: 371 us
  blocking collectives  193 us (52%)
  waiting for transfers between devices  115 us (31%)
  matrix products  27.3 us (7%)
  other arithmetic  17.8 us (5%)
  between operations  14.3 us (4%)
    all_gather x4, blocking collectives, pair_sum(): return lax.all_gather(matrices, 'pair').sum(0)  128 us
    all_gather x2, waiting for transfers between devices, aux_sum(): return lax.all_gather(mine, 'aux', axis=1, tiled=True)  115 us
    all_to_all x2, blocking collectives, aux_sum(): pieces = lax.all_to_all(pieces, 'aux', 1, 1, tiled=True)  65.7 us
    dot_general x6, matrix products, correlation_of(): lax.dot_general(first_rows, second_rows, (((1,), (1,)), ((), ())), precis...  12.8 us
    dot_general x4, matrix products, product(): jnp.dot(first_mat, second_mat, precision=HIGHEST_PRECISION, preferred_ele...  12 us
  transfers between devices with their start and end apart: 2, of which 2 were waited for; matrix products, arithmetic and copies ran while one was open for 2% of the time, Pallas kernels for 0%

commit v1 on v0

--- a/solution.py
+++ b/solution.py
@@ -33,7 +33,9 @@
     pieces = terms.reshape(rows, n_aux, cols // n_aux)
     pieces = lax.all_to_all(pieces, "aux", 1, 1, tiled=True)
     mine = pieces.astype(jnp.float32).sum(1)
-    return lax.all_gather(mine, "aux", axis=1, tiled=True)
+    return jnp.concatenate(
+        lax.all_to_all(jnp.stack([mine] * lax.axis_size("aux")), "aux", 0, 0), axis=1
+    )
 
 
 def inverse_factor(gram_now):

time: 372 us -> 342 us (0.919)
  waiting for transfers between devices: 115 us -> 83.8 us
  starting transfers between devices: 0.08 us -> 25.4 us
  between operations: 14.3 us -> 0.91 us
  blocking collectives: 193 us -> 181 us
  local copies, waits for them, and re-layouts: 2.75 us -> 9.82 us
    all_gather x2 -> x0, waiting for transfers between devices: 115 us -> none  [aux_sum(): return lax.all_gather(mine, 'aux', axis=1, tiled=True)]
    all_to_all x0 -> x2, waiting for transfers between devices: none -> 83.8 us  [aux_sum(): lax.all_to_all(jnp.stack([mine] * lax.axis_size('aux')), 'aux', 0, 0)]
    all_to_all x0 -> x2, starting transfers between devices: none -> 25.4 us  [aux_sum(): lax.all_to_all(jnp.stack([mine] * lax.axis_size('aux')), 'aux', 0, 0)]
    all_gather x4, blocking collectives: 128 us -> 116 us  [pair_sum(): return lax.all_gather(matrices, 'pair').sum(0)]
where the time goes in v1:
time: 342 us; the launch traced here: 341 us
  blocking collectives  181 us (53%)
  waiting for transfers between devices  83.8 us (25%)
  starting transfers between devices  25.4 us (7%)
  matrix products  23.7 us (7%)
  other arithmetic  16.5 us (5%)
  local copies, waits for them, and re-layouts  9.82 us (3%)
    all_gather x4, blocking collectives, pair_sum(): return lax.all_gather(matrices, 'pair').sum(0)  116 us
    all_to_all x2, waiting for transfers between devices, aux_sum(): lax.all_to_all(jnp.stack([mine] * lax.axis_size('aux')), 'aux', 0, 0)  83.8 us
    all_to_all x2, blocking collectives, aux_sum(): pieces = lax.all_to_all(pieces, 'aux', 1, 1, tiled=True)  65.6 us
    all_to_all x2, starting transfers between devices, aux_sum(): lax.all_to_all(jnp.stack([mine] * lax.axis_size('aux')), 'aux', 0, 0)  25.4 us
    dot_general x4, matrix products, product(): jnp.dot(first_mat, second_mat, precision=HIGHEST_PRECISION, preferred_ele...  12.1 us
    dot_general x6, matrix products, correlation_of(): lax.dot_general(first_rows, second_rows, (((1,), (1,)), ((), ())), precis...  9.09 us
    another operation x6, other arithmetic, inverse_factor(): lower_tri = jnp.linalg.cholesky(gram_now)  7.19 us
  transfers between devices with their start and end apart: 2, of which 2 were waited for; matrix products, arithmetic and copies ran while one was open for 2% of the time, Pallas kernels for 0%

profile of v1, /device:TPU:1, one launch (start us, length us, event | category | flops | bytes accessed | tf_op | source)
XLA Modules:
  0.0 341.3 jit_solution(15371869226992699163)
XLA Ops:
  0.6 1.6 convolution_multiply_fusion.3
  2.7 2.0 fusion.19
  4.7 31.4 %all-gather.4 = f32[32,192,32]{1,2,0:T(8,128)} all-gather(f32[1,192,32]{1,2,0:T(8,128)S(1)} %maximum_bitcast_fusion), channel_id=2, replica_groups=mesh['aux'=16,'pair'=32] {'pair'}, dimensions={0}, use_global_device_ids=true | all-gather | bytes 811008 | tf_op jit(solution)/shard_map/all_gather | solution.py:27
  37.6 2.9 cholesky.44
  41.8 2.4 custom-call.6
  45.6 35.1 %all_to_all.20 = bf16[32,16,512]{2,0,1:T(8,128)(2,1)S(1)} all-to-all(bf16[32,16,512]{2,0,1:T(8,128)(2,1)S(1)} %bitcast.74), channel_id=1, replica_groups=mesh['aux'=16,'pair'=32] {'aux'}, dimensions={1} | all-to-all | bytes 1048576 | tf_op jit(solution)/shard_map/all_to_all | solution.py:34
  82.0 12.7 %all-to-all-start.1 = ((f32[16,32,512]{2,1,0:T(8,128)}), f32[16,32,512]{2,1,0:T(8,128)}, u32[]{:S(2)}, u32[]{:S(2)}) async-start(f32[16,32,512]{2,1,0:T(8,128)} %stack.4), calls=%async_computation.1 | async-start | bytes 2097152 | tf_op jit(solution)/shard_map/all_to_all | solution.py:37
  96.8 1.5 fusion.20
  98.3 41.7 %all-to-all-done.1 = f32[16,32,512]{2,1,0:T(8,128)} async-done(((f32[16,32,512]{2,1,0:T(8,128)}), f32[16,32,512]{2,1,0:T(8,128)}, u32[]{:S(2)}, u32[]{:S(2)}) %all-to-all-start.1) | async-done | bytes 1048608 | tf_op jit(solution)/shard_map/all_to_all | solution.py:37
  140.0 1.4 copy.30
  143.6 29.6 %all-gather.1 = f32[1024,32]{1,0:T(8,128)S(1)} all-gather(f32[32,32]{1,0:T(8,128)S(1)} %copy.15), channel_id=3, replica_groups=mesh['aux'=16,'pair'=32] {'pair'}, dimensions={0}, use_global_device_ids=true | all-gather | bytes 135168 | tf_op jit(solution)/shard_map/all_gather | solution.py:27
  173.2 3.0 fusion.1
  176.2 2.4 convolution_bitcast_fusion
  179.7 25.1 %all-gather.5 = f32[32,192,32]{1,2,0:T(8,128)} all-gather(f32[1,192,32]{1,2,0:T(8,128)S(1)} %maximum_bitcast_fusion.1), channel_id=4, replica_groups=mesh['aux'=16,'pair'=32] {'pair'}, dimensions={0}, use_global_device_ids=true | all-gather | bytes 811008 | tf_op jit(solution)/shard_map/all_gather | solution.py:27
  204.8 1.3 reduce_sum.57
  206.2 2.9 cholesky.55
  210.5 2.4 custom-call.7
  214.3 30.5 %all_to_all.21 = bf16[32,16,512]{2,0,1:T(8,128)(2,1)S(1)} all-to-all(bf16[32,16,512]{2,0,1:T(8,128)(2,1)S(1)} %bitcast.76), channel_id=1, replica_groups=mesh['aux'=16,'pair'=32] {'aux'}, dimensions={1} | all-to-all | bytes 1048576 | tf_op jit(solution)/shard_map/all_to_all | solution.py:34
  245.9 12.6 %all-to-all-start.3 = ((f32[16,32,512]{2,1,0:T(8,128)}), f32[16,32,512]{2,1,0:T(8,128)}, u32[]{:S(2)}, u32[]{:S(2)}) async-start(f32[16,32,512]{2,1,0:T(8,128)} %stack.5), calls=%async_computation.3 | async-start | bytes 2097152 | tf_op jit(solution)/shard_map/all_to_all | solution.py:37
  258.6 3.2 fusion.21
  261.8 42.1 %all-to-all-done.3 = f32[16,32,512]{2,1,0:T(8,128)} async-done(((f32[16,32,512]{2,1,0:T(8,128)}), f32[16,32,512]{2,1,0:T(8,128)}, u32[]{:S(2)}, u32[]{:S(2)}) %all-to-all-start.3) | async-done | bytes 1048608 | tf_op jit(solution)/shard_map/all_to_all | solution.py:37
  303.9 1.4 copy.31
  307.4 29.6 %all-gather.3 = f32[1024,32]{1,0:T(8,128)S(1)} all-gather(f32[32,32]{1,0:T(8,128)S(1)} %copy.21), channel_id=5, replica_groups=mesh['aux'=16,'pair'=32] {'pair'}, dimensions={0}, use_global_device_ids=true | all-gather | bytes 135168 | tf_op jit(solution)/shard_map/all_gather | solution.py:27
  337.0 4.3 %fusion.18 = (bf16[32,8192]{1,0:T(8,128)(2,1)}, f32[32,8192]{1,0:T(8,128)}) fusion(f32[32,8192]{1,0:T(8,128)} %fusion.21, f32[8192]{0:T(1024)S(1)} %dynamic_slice.3, f32[32,32]{1,0:T(8,128)S(1)} %reduce_sum.59, f32[32,8192]{1,0:T(8,128)} %bitcast.68), kind=kOutput, calls=%fused_computation.48 | convolution fusion | flops 102236160 | bytes 3706880 | tf_op jit(solution)/shard_map/dot_general | solution.py:21
  (57 shorter events, 17.1 us)
Async XLA Ops:
  0.6 2.1 copy-start
  45.6 49.1 %copy-start.8 = (f32[1024]{0:T(1024)S(1)}, f32[1024]{0:T(1024)}, u32[]{:S(2)}) copy-start(f32[1024]{0:T(1024)} %param.9) | copy-start | bytes 12292
  45.6 49.1 %copy-start.9 = (f32[256]{0:T(256)S(1)}, f32[256]{0:T(256)}, u32[]{:S(2)}) copy-start(f32[256]{0:T(256)} %param.8) | copy-start | bytes 3076
  82.0 14.9 %copy-start.4 = (bf16[32,8192]{1,0:T(8,128)(2,1)S(1)}, bf16[32,8192]{1,0:T(8,128)(2,1)}, u32[]{:S(2)}) copy-start(bf16[32,8192]{1,0:T(8,128)(2,1)} %param.10) | copy-start | bytes 1572868
  82.0 58.1 %all-to-all-start.1 = ((f32[16,32,512]{2,1,0:T(8,128)}), f32[16,32,512]{2,1,0:T(8,128)}, u32[]{:S(2)}, u32[]{:S(2)}) async-start(f32[16,32,512]{2,1,0:T(8,128)} %stack.4), calls=%async_computation.1 | async-start | bytes 2097152 | tf_op jit(solution)/shard_map/all_to_all | solution.py:37
  140.0 2.4 copy-start.3
  141.4 1.0 copy-start.6
  176.2 3.4 %copy-start.1 = (f32[32,8192]{1,0:T(8,128)}, f32[32,8192]{1,0:T(8,128)S(1)}, u32[]{:S(2)}) copy-start(f32[32,8192]{1,0:T(8,128)S(1)} %fusion.1) | copy-start | bytes 3145732
  245.9 57.9 %all-to-all-start.3 = ((f32[16,32,512]{2,1,0:T(8,128)}), f32[16,32,512]{2,1,0:T(8,128)}, u32[]{:S(2)}, u32[]{:S(2)}) async-start(f32[16,32,512]{2,1,0:T(8,128)} %stack.5), calls=%async_computation.3 | async-start | bytes 2097152 | tf_op jit(solution)/shard_map/all_to_all | solution.py:37
  303.9 2.4 copy-start.2
  305.3 1.0 copy-start.5
  337.0 4.3 %copy-start.7 = (f32[32,32]{1,0:T(8,128)}, f32[32,32]{1,0:T(8,128)S(1)}, u32[]{:S(2)}) copy-start(f32[32,32]{1,0:T(8,128)S(1)} %reduce_sum.59) | copy-start | bytes 12292
